TPU v7x, 256 devices: a whole 4x4x8 slice. The times are simulated.
256 devices in a mesh: grp: 32 (over z, y_hi, core), tp: 8 (over y_lo, x).
Axes of the slice: x: 4, y: 4 (y_hi: 2, y_lo: 2; y = y_hi * 2 + y_lo), z: 8, core: 2. Of those that a mesh axis runs over, the one named last changes fastest.
Arguments:
- states_in: bfloat16 [16384, 1536], P('grp', 'tp'), may hold values from -6 to 6
- segment_ids: int32 [16384], P('grp'), may hold values from 0 to 223, as said below
- positions: int32 [16384], P('grp'), may hold values from 0 to 1009, as said below
- attention_gain: bfloat16 [1536], P('tp'), may hold values from 0.5 to 1.5
- feedforward_gain: bfloat16 [1536], P('tp'), may hold values from 0.5 to 1.5
- query_weight: bfloat16 [1536, 1536], P('grp', 'tp'), may hold values from -1 to 1
- keyvalue_weight: bfloat16 [1536, 8, 128], P('grp', 'tp'), may hold values from -128 to 128
- output_weight: bfloat16 [1536, 1536], P('tp'), may hold values from -0.15625 to 0.15625
- route_experts: int32 [16384, 8], P('grp'), may hold values from 0 to 19, all different within a row; in each aligned block of 512 rows (0 to 511, 512 to 1023, ...) at most 256 rows name the same one
- route_weights: float32 [16384, 8], P('grp'), may hold values from 0.05 to 0.3
- expert_gateup: bfloat16 [40, 1536, 512], P('tp'), may hold values from -0.15625 to 0.15625
- expert_down: bfloat16 [40, 256, 1536], P('tp'), may hold values from -0.25 to 0.25
- cache_slots: int32 [16384], P('grp'), may hold values from 0 to 16383, as said below
Outputs:
- layer_output: bfloat16 [16384, 1536], P('grp', 'tp')
- paged_cache: bfloat16 [16384, 8, 128], P('grp', 'tp')
- log_sums: float32 [24, 16384], P('tp', 'grp')
Inputs may be any that keep to these rules, and one draw needn't show every extreme that they name: `segment_ids`: equal ids mark the tokens of one prompt; the tokens of a prompt lie within one pair of groups 2p and 2p+1. `positions`: positions count from 0 within each prompt; one prompt of groups 0 and 1 has 2 * (505) tokens. `route_experts`: each row names 8 different experts; at most 256 rows of one group name the same expert, and that number is reached. `cache_slots`: every cache row is named once; the tokens of each group fill exactly 16 rows of every group's block of 512 rows.
All inputs are finite; a program needn't handle non-finite values.
Results may differ from a plain program's by a relative error of at most 0.01.
The roundings to bfloat16 on the way count: a program that leaves them out, or rounds other values in their place, can miss the bound.
Values may be sent and summed in bfloat16 or wider, within the bound.
No kernel may reach another device: no remote copies, remote signals or barrier semaphores. Data moves between devices by JAX's collectives and lax.ppermute only.
A program may use at most 128 MiB of HBM per device.

v0:
```python
import jax
import jax.numpy as jnp
from jax import lax
from jax.sharding import Mesh
from jax.sharding import PartitionSpec as P

HD = 64
attn_scale = 0.015625
norm_eps = 1e-06
rope_base = 10000.0
G = ("z", "yh", "c")
T = ("yl", "x")


def rms_scale(values, gain_row):
    floats = values.astype(jnp.float32)
    mean_square = jnp.mean(floats * floats, axis=-1, keepdims=True)
    return (floats * lax.rsqrt(mean_square + norm_eps) * gain_row.astype(jnp.float32)).astype(
        jnp.bfloat16
    )


def rotate(values, places):
    half_width = values.shape[-1] // 2
    frequency = rope_base ** (-jnp.arange(half_width, dtype=jnp.float32) * 2.0 / values.shape[-1])
    angles = places.astype(jnp.float32)[:, None] * frequency[None, :]
    cosine = jnp.cos(angles)[:, None, :]
    sine_part = jnp.sin(angles)[:, None, :]
    leading = values[..., :half_width]
    trailing = values[..., half_width:]
    return jnp.concatenate(
        [leading * cosine - trailing * sine_part, trailing * cosine + leading * sine_part], axis=-1
    )


def attend_block(query_block, seg_block, pos_block, all_rows, all_seg, all_pos):
    key_part = all_rows[..., :HD]
    value_part = all_rows[..., HD:]
    scores = (
        jnp.einsum("qgrd,kgd->grqk", query_block, key_part, preferred_element_type=jnp.float32)
        * attn_scale
    )
    allowed = (seg_block[:, None] == all_seg[None, :]) & (all_pos[None, :] <= pos_block[:, None])
    masked = jnp.where(allowed, scores, -jnp.inf)
    row_peak = jnp.max(masked, axis=-1, keepdims=True)
    exponent = jnp.exp(masked - row_peak)
    row_total = jnp.sum(exponent, axis=-1, keepdims=True)
    log_total = (row_peak + jnp.log(row_total))[..., 0]
    weights_low = (exponent / row_total).astype(jnp.bfloat16)
    mixed_rows = jnp.einsum(
        "grqk,kgd->qgrd", weights_low, value_part, preferred_element_type=jnp.float32
    )
    return (mixed_rows.astype(jnp.bfloat16), log_total)


def expert_terms(normed, route_experts, route_weights, gateup, down, slot_first):
    local_experts = gateup.shape[0]
    half_units = down.shape[1]
    owned_experts = slot_first + jnp.arange(local_experts, dtype=jnp.int32)
    matches = route_experts[:, :, None] == owned_experts[None, None, :]
    route_scale = jnp.sum(jnp.where(matches, route_weights[:, :, None], 0.0), axis=1)
    gate_up = jnp.einsum("td,edf->etf", normed, gateup, preferred_element_type=jnp.float32)
    activated = (jax.nn.silu(gate_up[..., :half_units]) * gate_up[..., half_units:]).astype(
        jnp.bfloat16
    )
    produced = jnp.einsum("etf,efd->etd", activated, down, preferred_element_type=jnp.float32)
    return jnp.sum(route_scale.T[:, :, None] * produced, axis=0)


def gather_rows_over_groups(block):
    width = block.shape[1]
    ci = lax.axis_index("c")
    other_c = lax.ppermute(block, "c", [(0, 1), (1, 0)])
    cfull = jnp.where(ci == 0, jnp.stack([block, other_c]), jnp.stack([other_c, block]))
    yi = lax.axis_index("yh")
    other_y = lax.ppermute(cfull, "yh", [(0, 1), (1, 0)])
    yfull = jnp.where(yi == 0, jnp.stack([cfull, other_y]), jnp.stack([other_y, cfull]))
    nz = lax.axis_size("z")
    zi = lax.axis_index("z")
    got = [yfull]
    for k in range(1, nz):
        got.append(lax.ppermute(yfull, "z", [(i, (i + k) % nz) for i in range(nz)]))
    stacked = jnp.stack(got)
    zfull = jnp.take(stacked, (zi - jnp.arange(nz)) % nz, axis=0)
    return zfull.reshape(-1, width)


def place_cache_rows(own_rows, cache_slots, group_rank):
    tokens, keyvalue_heads, row_width = own_rows.shape
    width = keyvalue_heads * row_width
    group_count = lax.axis_size(G)
    per_owner = tokens // group_count
    sequence = jnp.arange(tokens, dtype=jnp.int32)
    owners = cache_slots // tokens
    owner_hot = (owners[:, None] == jnp.arange(group_count, dtype=jnp.int32)[None, :]).astype(
        jnp.bfloat16
    )
    earlier = (sequence[:, None] > sequence[None, :]).astype(jnp.bfloat16)
    before = jnp.dot(earlier, owner_hot, preferred_element_type=jnp.float32)
    rank = jnp.sum(before * owner_hot.astype(jnp.float32), axis=1).astype(jnp.int32)
    place = owners * per_owner + rank
    moving = (place[None, :] == sequence[:, None]).astype(jnp.bfloat16)
    digits = jnp.stack([cache_slots // 128, cache_slots % 128], axis=1).astype(jnp.bfloat16)
    payload = jnp.concatenate([own_rows.reshape(tokens, width), digits], axis=1)
    sent = jnp.dot(moving, payload, preferred_element_type=jnp.float32).astype(jnp.bfloat16)
    sent_rows = sent[:, :width].reshape(group_count, per_owner, width)
    sent_digits = sent[:, width:].reshape(group_count, per_owner, 2).transpose(0, 2, 1)
    digit_row = jnp.zeros((group_count, 1, width), jnp.bfloat16)
    digit_row = lax.dynamic_update_slice(
        digit_row, sent_digits.reshape(group_count, 1, 2 * per_owner), (0, 0, 0)
    )
    packet = jnp.concatenate([sent_rows, digit_row], axis=1)
    got = lax.all_to_all(packet, G, 0, 0, tiled=True)
    got_rows = got[:, :per_owner, :].reshape(tokens, width)
    got_digits = (
        got[:, per_owner, : 2 * per_owner].astype(jnp.int32).reshape(group_count, 2, per_owner)
    )
    got_slots = (got_digits[:, 0, :] * 128 + got_digits[:, 1, :]).reshape(tokens)
    targets = got_slots - group_rank * tokens
    landing = (targets[None, :] == sequence[:, None]).astype(jnp.bfloat16)
    placed = jnp.dot(landing, got_rows, preferred_element_type=jnp.float32).astype(jnp.bfloat16)
    return placed.reshape(tokens, keyvalue_heads, row_width)


def shards(
    states_in,
    segment_ids,
    positions,
    attention_gain,
    feedforward_gain,
    query_weight,
    keyvalue_weight,
    output_weight,
    route_experts,
    route_weights,
    expert_gateup,
    expert_down,
    cache_slots,
):
    tokens = states_in.shape[0]
    width_share = states_in.shape[1]
    head_rank = lax.axis_index(T)
    group_rank = lax.axis_index(G)
    gain_rows = jnp.zeros((8, width_share), states_in.dtype)
    gain_rows = gain_rows.at[0].set(attention_gain).at[1].set(feedforward_gain)
    packed = jnp.concatenate([states_in, gain_rows], axis=0)
    packed_full = lax.all_gather(packed, T, axis=1, tiled=True)
    states_full = packed_full[:tokens]
    gain_attend = packed_full[tokens]
    gain_forward = packed_full[tokens + 1]
    normed_in = rms_scale(states_full, gain_attend)
    query_cols = query_weight.shape[1]
    keyvalue_heads = keyvalue_weight.shape[1]
    heads_local = query_cols // HD
    piece_rows = query_weight.shape[0]
    weights_packed = jnp.concatenate(
        [query_weight, keyvalue_weight.reshape(piece_rows, -1)], axis=1
    )
    weights_full = gather_rows_over_groups(weights_packed)
    query_full_w = weights_full[:, :query_cols]
    keyvalue_full_w = weights_full[:, query_cols:]
    query_sum = jnp.dot(normed_in, query_full_w, preferred_element_type=jnp.float32)
    keyvalue_sum = jnp.dot(normed_in, keyvalue_full_w, preferred_element_type=jnp.float32)
    queries = rotate(query_sum.reshape(tokens, heads_local, HD), positions).astype(jnp.bfloat16)
    keyvalue_sum = keyvalue_sum.reshape(tokens, keyvalue_heads, 2 * HD)
    key_rows = rotate(keyvalue_sum[..., :HD], positions).astype(jnp.bfloat16)
    value_rows = keyvalue_sum[..., HD:].astype(jnp.bfloat16)
    own_rows = jnp.concatenate([key_rows, value_rows], axis=-1)
    other_rows, other_seg, other_pos = lax.ppermute(
        (own_rows, segment_ids, positions), "c", [(0, 1), (1, 0)]
    )
    all_rows = jnp.concatenate([own_rows, other_rows], axis=0)
    all_seg = jnp.concatenate([segment_ids, other_seg], axis=0)
    all_pos = jnp.concatenate([positions, other_pos], axis=0)
    group_ratio = heads_local // keyvalue_heads
    query_block = queries.reshape(tokens, keyvalue_heads, group_ratio, HD)
    mixed, log_part = attend_block(query_block, segment_ids, positions, all_rows, all_seg, all_pos)
    attended = mixed.reshape(tokens, heads_local * HD)
    log_sums = log_part.reshape(heads_local, tokens)
    partial_value = jnp.dot(attended, output_weight, preferred_element_type=jnp.float32)
    tp_count = lax.axis_size(T)
    value_parts = (
        partial_value.astype(jnp.bfloat16).reshape(tokens, tp_count, width_share).transpose(1, 0, 2)
    )
    value_got = lax.all_to_all(value_parts, T, 0, 0, tiled=True)
    summed_share = jnp.sum(value_got.astype(jnp.float32), axis=0)
    residual_share = (states_in.astype(jnp.float32) + summed_share).astype(jnp.bfloat16)
    residual_share, own_rows, cache_slots = lax.optimization_barrier(
        (residual_share, own_rows, cache_slots)
    )
    residual = lax.all_gather(residual_share, T, axis=1, tiled=True)
    paged_rows = place_cache_rows(own_rows, cache_slots, group_rank)
    residual, paged_rows = lax.optimization_barrier((residual, paged_rows))
    normed = rms_scale(residual, gain_forward)
    slot_first = head_rank // 2 * expert_gateup.shape[0]
    terms = expert_terms(
        normed, route_experts, route_weights, expert_gateup, expert_down, slot_first
    )
    term_parts = (
        terms.astype(jnp.bfloat16).reshape(tokens, tp_count, width_share).transpose(1, 0, 2)
    )
    term_got = lax.all_to_all(term_parts, T, 0, 0, tiled=True)
    expert_share = jnp.sum(term_got.astype(jnp.float32), axis=0)
    layer_output = (residual_share.astype(jnp.float32) + expert_share).astype(jnp.bfloat16)
    return (layer_output, paged_rows, log_sums)


def solution(mesh):
    fine = Mesh(mesh.devices.reshape(8, 2, 2, 2, 4), ("z", "yh", "c", "yl", "x"))
    return jax.shard_map(
        shards,
        mesh=fine,
        in_specs=(
            P(G, T),
            P(G),
            P(G),
            P(T),
            P(T),
            P(G, T),
            P(G, T, None),
            P(T, None),
            P(G, None),
            P(G, None),
            P(T, None, None),
            P(T, None, None),
            P(G),
        ),
        out_specs=(P(G, T), P(G, T, None), P(T, G)),
        check_vma=False,
    )
```

profile of v0, /device:TPU:32, one launch (start us, length us, event | category | flops | bytes accessed | tf_op | source)
XLA Modules:
  0.0 187.5 jit_solution(6620179228807870160)
XLA Ops:
  9.7 1.7 pad_maximum_fusion.1
  17.0 3.3 %collective-permute-start.1 = (bf16[2,48,320]{2,1,0:T(8,128)(2,1)S(1)}, bf16[2,48,320]{2,1,0:T(8,128)(2,1)S(1)}, u32[]{:S(2)}, u32[]{:S(2)}) collective-permute-start(bf16[2,48,320]{2,1,0:T(8,128)(2,1)S(1)} %maximum_select_fusion.3), channel_id=1, source_target_pairs={{0,16},{16,0},{1,17},{17,1},{2,18},{18,2},{3,19},{19,3},{4,20},{20... | collective-permute-start | bytes 184328 | tf_op jit(solution)/shard_map/ppermute | solution.py:76
  20.3 2.9 %collective-permute-done.1 = bf16[2,48,320]{2,1,0:T(8,128)(2,1)S(1)} collective-permute-done((bf16[2,48,320]{2,1,0:T(8,128)(2,1)S(1)}, bf16[2,48,320]{2,1,0:T(8,128)(2,1)S(1)}, u32[]{:S(2)}, u32[]{:S(2)}) %collective-permute-start.1) | collective-permute-done | bytes 61472 | tf_op jit(solution)/shard_map/ppermute | solution.py:76
  23.2 2.0 %collective-permute-start.2 = (bf16[2,2,48,320]{3,2,1,0:T(8,128)(2,1)S(1)}, bf16[2,2,48,320]{3,2,1,0:T(8,128)(2,1)S(1)}, u32[]{:S(2)}, u32[]{:S(2)}) collective-permute-start(bf16[2,2,48,320]{3,2,1,0:T(8,128)(2,1)S(1)} %maximum_select_fusion.1), channel_id=1, source_target_pairs={{0,32},{32,64},{64,96},{96,128},{128,160},{160,192},{192,224},{224... | collective-permute-start | bytes 368648 | tf_op jit(solution)/shard_map/ppermute | solution.py:82
  25.2 4.6 %collective-permute-start.3 = (bf16[2,2,48,320]{3,2,1,0:T(8,128)(2,1)S(1)}, bf16[2,2,48,320]{3,2,1,0:T(8,128)(2,1)S(1)}, u32[]{:S(2)}, u32[]{:S(2)}) collective-permute-start(bf16[2,2,48,320]{3,2,1,0:T(8,128)(2,1)S(1)} %maximum_select_fusion.1), channel_id=1, source_target_pairs={{0,64},{32,96},{64,128},{96,160},{128,192},{160,224},{192,0},{224,... | collective-permute-start | bytes 368648 | tf_op jit(solution)/shard_map/ppermute | solution.py:82
  29.8 1.9 %collective-permute-start.4 = (bf16[2,2,48,320]{3,2,1,0:T(8,128)(2,1)S(1)}, bf16[2,2,48,320]{3,2,1,0:T(8,128)(2,1)S(1)}, u32[]{:S(2)}, u32[]{:S(2)}) collective-permute-start(bf16[2,2,48,320]{3,2,1,0:T(8,128)(2,1)S(1)} %maximum_select_fusion.1), channel_id=1, source_target_pairs={{0,96},{32,128},{64,160},{96,192},{128,224},{160,0},{192,32},{224,... | collective-permute-start | bytes 368648 | tf_op jit(solution)/shard_map/ppermute | solution.py:82
  33.2 3.0 %collective-permute-start.6 = (bf16[2,2,48,320]{3,2,1,0:T(8,128)(2,1)S(1)}, bf16[2,2,48,320]{3,2,1,0:T(8,128)(2,1)S(1)}, u32[]{:S(2)}, u32[]{:S(2)}) collective-permute-start(bf16[2,2,48,320]{3,2,1,0:T(8,128)(2,1)S(1)} %maximum_select_fusion.1), channel_id=1, source_target_pairs={{0,160},{32,192},{64,224},{96,0},{128,32},{160,64},{192,96},{224,1... | collective-permute-start | bytes 368648 | tf_op jit(solution)/shard_map/ppermute | solution.py:82
  36.3 2.5 %collective-permute-start.7 = (bf16[2,2,48,320]{3,2,1,0:T(8,128)(2,1)S(1)}, bf16[2,2,48,320]{3,2,1,0:T(8,128)(2,1)S(1)}, u32[]{:S(2)}, u32[]{:S(2)}) collective-permute-start(bf16[2,2,48,320]{3,2,1,0:T(8,128)(2,1)S(1)} %maximum_select_fusion.1), channel_id=1, source_target_pairs={{0,192},{32,224},{64,0},{96,32},{128,64},{160,96},{192,128},{224,1... | collective-permute-start | bytes 368648 | tf_op jit(solution)/shard_map/ppermute | solution.py:82
  40.1 3.8 %collective-permute-start.8 = (bf16[2,2,48,320]{3,2,1,0:T(8,128)(2,1)S(1)}, bf16[2,2,48,320]{3,2,1,0:T(8,128)(2,1)S(1)}, u32[]{:S(2)}, u32[]{:S(2)}) collective-permute-start(bf16[2,2,48,320]{3,2,1,0:T(8,128)(2,1)S(1)} %maximum_select_fusion.1), channel_id=1, source_target_pairs={{0,224},{32,0},{64,32},{96,64},{128,96},{160,128},{192,160},{224,1... | collective-permute-start | bytes 368648 | tf_op jit(solution)/shard_map/ppermute | solution.py:82
  43.9 9.9 %collective-permute-done.4 = bf16[2,2,48,320]{3,2,1,0:T(8,128)(2,1)S(1)} collective-permute-done((bf16[2,2,48,320]{3,2,1,0:T(8,128)(2,1)S(1)}, bf16[2,2,48,320]{3,2,1,0:T(8,128)(2,1)S(1)}, u32[]{:S(2)}, u32[]{:S(2)}) %collective-permute-start.4) | collective-permute-done | bytes 122912 | tf_op jit(solution)/shard_map/ppermute | solution.py:82
  54.0 6.0 %collective-permute-done.7 = bf16[2,2,48,320]{3,2,1,0:T(8,128)(2,1)S(1)} collective-permute-done((bf16[2,2,48,320]{3,2,1,0:T(8,128)(2,1)S(1)}, bf16[2,2,48,320]{3,2,1,0:T(8,128)(2,1)S(1)}, u32[]{:S(2)}, u32[]{:S(2)}) %collective-permute-start.7) | collective-permute-done | bytes 122912 | tf_op jit(solution)/shard_map/ppermute | solution.py:82
  62.7 1.9 %fusion.2 = f32[512]{0:T(512)S(1)} fusion(bf16[520,1536]{0,1:T(8,128)(2,1)} %all-gather.3.cloned.1.call-done), kind=kLoop, calls=%fused_computation.11 | loop fusion | flops 2358784 | bytes 1574912 | tf_op jit(solution)/shard_map/reduce_sum | solution.py:17
  71.9 2.0 %fusion.17 = bf16[64,3,512]{2,0,1:T(8,128)(2,1)S(1)} fusion(f32[3,512]{1,0:T(4,128)S(1)} %fusion, f32[3,512]{1,0:T(4,128)S(1)} %get-tuple-element.51, f32[1024,512,3]{1,0,2:T(8,128)S(1)} %get-tuple-element.52, pred[512,1024]{0,1:T(8,128)(4,1)S(1)} %compare_and_fusion, bf16[1024,1,128]{0,2,1:T(8,128)(2,1)S(1)} %pad_maximum_fusion), kind=kOutput, calls=%fused_computation.31 | convolution fusion | flops 209289216 | bytes 7159808 | tf_op jit(solution)/shard_map/grqk,kgd->qgrd/dot_general | solution.py:50
  74.5 1.6 copy.67
  76.1 27.0 %all_to_all.15 = bf16[8,512,192]{1,2,0:T(8,128)(2,1)S(1)} all-to-all(bf16[8,512,192]{1,2,0:T(8,128)(2,1)} %bitcast.96), channel_id=1, replica_groups=mesh['z'=8,'yh'=2,'c'=2,'yl'=2,'x'=4] {'yl','x'}, dimensions={0} | all-to-all | bytes 3145728 | tf_op jit(solution)/shard_map/all_to_all | solution.py:185
  106.0 6.6 %all-to-all-start.1 = ((bf16[32,17,128]{2,1,0:T(8,128)(2,1)}), bf16[32,17,128]{2,1,0:T(8,128)(2,1)S(1)}, u32[]{:S(2)}, u32[]{:S(2)}) async-start(bf16[32,17,128]{2,1,0:T(8,128)(2,1)} %fusion.30), calls=%async_computation.1 | async-start | bytes 393216 | tf_op jit(solution)/shard_map/all_to_all | solution.py:113
  112.7 11.6 %all-to-all-done.1 = bf16[32,17,128]{2,1,0:T(8,128)(2,1)S(1)} async-done(((bf16[32,17,128]{2,1,0:T(8,128)(2,1)}), bf16[32,17,128]{2,1,0:T(8,128)(2,1)S(1)}, u32[]{:S(2)}, u32[]{:S(2)}) %all-to-all-start.1) | async-done | bytes 139296 | tf_op jit(solution)/shard_map/all_to_all | solution.py:113
  125.6 17.9 %all-gather.5.cloned.1.call-done = bf16[512,1536]{0,1:T(8,128)(2,1)} async-done(((bf16[512,192]{0,1:T(8,128)(2,1)}), bf16[512,1536]{0,1:T(8,128)(2,1)}) %all-gather.5.cloned.1.call-update) | async-done | bytes 1572880 | tf_op jit(solution)/shard_map/all_gather | solution.py:191
  143.5 1.8 fusion.5
  145.3 8.7 %convolution_bitcast_fusion = f32[5,512,512]{2,1,0:T(8,128)S(1)} fusion(bf16[5,1536,512]{2,1,0:T(8,128)(2,1)} %param.27, bf16[512,1536]{0,1:T(8,128)(2,1)} %all-gather.5.cloned.1.call-done, f32[1536]{0:T(1024)S(1)} %get-tuple-element.37, f32[512]{0:T(512)S(1)} %add_rsqrt_fusion), kind=kOutput, calls=%fused_computation.24 | convolution fusion | flops 4029677568 | bytes 14688256 | tf_op jit(solution)/shard_map/td,edf->etf/dot_general | solution.py:62
  154.0 3.5 %multiply_reduce_fusion = bf16[512,1536]{1,0:T(8,128)(2,1)S(1)} fusion(bf16[5,256,1536]{2,1,0:T(8,128)(2,1)S(1)} %copy-done.8, f32[5,512]{1,0:T(8,128)S(1)} %bitcast.110, f32[5,512,512]{2,1,0:T(8,128)S(1)} %convolution_bitcast_fusion), kind=kOutput, calls=%fused_computation.1 | convolution fusion | flops 2024275968 | bytes 10758144 | tf_op jit(solution)/shard_map/etf,efd->etd/dot_general | solution.py:66
  157.5 1.6 copy.75
  159.1 3.7 %all-to-all-start.2 = ((bf16[8,512,192]{1,2,0:T(8,128)(2,1)}), bf16[8,512,192]{1,2,0:T(8,128)(2,1)S(1)}, u32[]{:S(2)}, u32[]{:S(2)}) async-start(bf16[8,512,192]{1,2,0:T(8,128)(2,1)} %bitcast.42), calls=%async_computation.2 | async-start | bytes 3145728 | tf_op jit(solution)/shard_map/all_to_all | solution.py:202
  163.4 16.3 %all-to-all-done.2 = bf16[8,512,192]{1,2,0:T(8,128)(2,1)S(1)} async-done(((bf16[8,512,192]{1,2,0:T(8,128)(2,1)}), bf16[8,512,192]{1,2,0:T(8,128)(2,1)S(1)}, u32[]{:S(2)}, u32[]{:S(2)}) %all-to-all-start.2) | async-done | bytes 1572896 | tf_op jit(solution)/shard_map/all_to_all | solution.py:202
  (109 shorter events, 27.1 us)
Async XLA Ops:
  7.2 66.7 %copy-start = (bf16[192,1536]{1,0:T(8,128)(2,1)S(1)}, bf16[192,1536]{1,0:T(8,128)(2,1)}, u32[]{:S(2)}) copy-start(bf16[192,1536]{1,0:T(8,128)(2,1)} %param.24) | copy-start | bytes 1769476
  7.2 55.5 %all-gather.3.cloned.1.call-start = ((), (), s32[]{:S(2)}) async-start(), calls=%async_computation.3 | async-start | bytes 2211840 | tf_op jit(solution)/shard_map/all_gather | solution.py:147
  8.1 8.8 %collective-permute-start = (bf16[48,320]{1,0:T(8,128)(2,1)S(1)}, bf16[48,320]{1,0:T(8,128)(2,1)S(1)}, u32[]{:S(2)}, u32[]{:S(2)}) collective-permute-start(bf16[48,320]{1,0:T(8,128)(2,1)S(1)} %get-tuple-element.45), channel_id=1, source_target_pairs={{0,8},{8,0},{1,9},{9,1},{2,10},{10,2},{3,11},{11,3},{4,12},{12,4},... | collective-permute-start | bytes 92168 | tf_op jit(solution)/shard_map/ppermute | solution.py:73
  11.4 132.0 %all-gather.5.cloned.1.call-start = ((), (), s32[]{:S(2)}) async-start(), calls=%async_computation.4 | async-start | bytes 1769472 | tf_op jit(solution)/shard_map/all_gather | solution.py:191
  11.5 2.5 %collective-permute-start.10 = (s32[512]{0:T(512)}, s32[512]{0:T(512)S(1)}, u32[]{:S(2)}, u32[]{:S(2)}) collective-permute-start(s32[512]{0:T(512)} %param.18), channel_id=1, source_target_pairs={{0,8},{8,0},{1,9},{9,1},{2,10},{10,2},{3,11},{11,3},{4,12},{12,4},... | collective-permute-start | bytes 6152 | tf_op jit(solution)/shard_map/ppermute | solution.py:169
  12.1 2.7 %collective-permute-start.11 = (s32[512]{0:T(512)}, s32[512]{0:T(512)S(1)}, u32[]{:S(2)}, u32[]{:S(2)}) collective-permute-start(s32[512]{0:T(512)} %param.19), channel_id=1, source_target_pairs={{0,8},{8,0},{1,9},{9,1},{2,10},{10,2},{3,11},{11,3},{4,12},{12,4},... | collective-permute-start | bytes 6152 | tf_op jit(solution)/shard_map/ppermute | solution.py:169
  17.0 6.2 %collective-permute-start.1 = (bf16[2,48,320]{2,1,0:T(8,128)(2,1)S(1)}, bf16[2,48,320]{2,1,0:T(8,128)(2,1)S(1)}, u32[]{:S(2)}, u32[]{:S(2)}) collective-permute-start(bf16[2,48,320]{2,1,0:T(8,128)(2,1)S(1)} %maximum_select_fusion.3), channel_id=1, source_target_pairs={{0,16},{16,0},{1,17},{17,1},{2,18},{18,2},{3,19},{19,3},{4,20},{20... | collective-permute-start | bytes 184328 | tf_op jit(solution)/shard_map/ppermute | solution.py:76
  23.2 13.0 %collective-permute-start.2 = (bf16[2,2,48,320]{3,2,1,0:T(8,128)(2,1)S(1)}, bf16[2,2,48,320]{3,2,1,0:T(8,128)(2,1)S(1)}, u32[]{:S(2)}, u32[]{:S(2)}) collective-permute-start(bf16[2,2,48,320]{3,2,1,0:T(8,128)(2,1)S(1)} %maximum_select_fusion.1), channel_id=1, source_target_pairs={{0,32},{32,64},{64,96},{96,128},{128,160},{160,192},{192,224},{224... | collective-permute-start | bytes 368648 | tf_op jit(solution)/shard_map/ppermute | solution.py:82
  25.2 14.8 %collective-permute-start.3 = (bf16[2,2,48,320]{3,2,1,0:T(8,128)(2,1)S(1)}, bf16[2,2,48,320]{3,2,1,0:T(8,128)(2,1)S(1)}, u32[]{:S(2)}, u32[]{:S(2)}) collective-permute-start(bf16[2,2,48,320]{3,2,1,0:T(8,128)(2,1)S(1)} %maximum_select_fusion.1), channel_id=1, source_target_pairs={{0,64},{32,96},{64,128},{96,160},{128,192},{160,224},{192,0},{224,... | collective-permute-start | bytes 368648 | tf_op jit(solution)/shard_map/ppermute | solution.py:82
  29.8 24.0 %collective-permute-start.4 = (bf16[2,2,48,320]{3,2,1,0:T(8,128)(2,1)S(1)}, bf16[2,2,48,320]{3,2,1,0:T(8,128)(2,1)S(1)}, u32[]{:S(2)}, u32[]{:S(2)}) collective-permute-start(bf16[2,2,48,320]{3,2,1,0:T(8,128)(2,1)S(1)} %maximum_select_fusion.1), channel_id=1, source_target_pairs={{0,96},{32,128},{64,160},{96,192},{128,224},{160,0},{192,32},{224,... | collective-permute-start | bytes 368648 | tf_op jit(solution)/shard_map/ppermute | solution.py:82
  31.7 22.2 %collective-permute-start.5 = (bf16[2,2,48,320]{3,2,1,0:T(8,128)(2,1)S(1)}, bf16[2,2,48,320]{3,2,1,0:T(8,128)(2,1)S(1)}, u32[]{:S(2)}, u32[]{:S(2)}) collective-permute-start(bf16[2,2,48,320]{3,2,1,0:T(8,128)(2,1)S(1)} %maximum_select_fusion.1), channel_id=1, source_target_pairs={{0,128},{32,160},{64,192},{96,224},{128,0},{160,32},{192,64},{224,... | collective-permute-start | bytes 368648 | tf_op jit(solution)/shard_map/ppermute | solution.py:82
  33.2 20.8 %collective-permute-start.6 = (bf16[2,2,48,320]{3,2,1,0:T(8,128)(2,1)S(1)}, bf16[2,2,48,320]{3,2,1,0:T(8,128)(2,1)S(1)}, u32[]{:S(2)}, u32[]{:S(2)}) collective-permute-start(bf16[2,2,48,320]{3,2,1,0:T(8,128)(2,1)S(1)} %maximum_select_fusion.1), channel_id=1, source_target_pairs={{0,160},{32,192},{64,224},{96,0},{128,32},{160,64},{192,96},{224,1... | collective-permute-start | bytes 368648 | tf_op jit(solution)/shard_map/ppermute | solution.py:82
  36.3 23.7 %collective-permute-start.7 = (bf16[2,2,48,320]{3,2,1,0:T(8,128)(2,1)S(1)}, bf16[2,2,48,320]{3,2,1,0:T(8,128)(2,1)S(1)}, u32[]{:S(2)}, u32[]{:S(2)}) collective-permute-start(bf16[2,2,48,320]{3,2,1,0:T(8,128)(2,1)S(1)} %maximum_select_fusion.1), channel_id=1, source_target_pairs={{0,192},{32,224},{64,0},{96,32},{128,64},{160,96},{192,128},{224,1... | collective-permute-start | bytes 368648 | tf_op jit(solution)/shard_map/ppermute | solution.py:82
  40.1 21.4 %collective-permute-start.8 = (bf16[2,2,48,320]{3,2,1,0:T(8,128)(2,1)S(1)}, bf16[2,2,48,320]{3,2,1,0:T(8,128)(2,1)S(1)}, u32[]{:S(2)}, u32[]{:S(2)}) collective-permute-start(bf16[2,2,48,320]{3,2,1,0:T(8,128)(2,1)S(1)} %maximum_select_fusion.1), channel_id=1, source_target_pairs={{0,224},{32,0},{64,32},{96,64},{128,96},{160,128},{192,160},{224,1... | collective-permute-start | bytes 368648 | tf_op jit(solution)/shard_map/ppermute | solution.py:82
  62.7 3.5 %copy-start.1 = (bf16[520,1536]{0,1:T(8,128)(2,1)S(1)}, bf16[520,1536]{0,1:T(8,128)(2,1)}, u32[]{:S(2)}) copy-start(bf16[520,1536]{0,1:T(8,128)(2,1)} %all-gather.3.cloned.1.call-done) | copy-start | bytes 4792324
  67.4 1.1 copy-start.4
  67.5 1.6 collective-permute-start.9
  76.1 27.2 %copy-start.3 = (bf16[512,192]{0,1:T(8,128)(2,1)S(1)}, bf16[512,192]{0,1:T(8,128)(2,1)}, u32[]{:S(2)}) copy-start(bf16[512,192]{0,1:T(8,128)(2,1)} %param.17) | copy-start | bytes 589828
  103.4 9.2 %copy-start.5 = (f32[512,8]{0,1:T(8,128)S(1)}, f32[512,8]{0,1:T(8,128)}, u32[]{:S(2)}) copy-start(f32[512,8]{0,1:T(8,128)} %param.26) | copy-start | bytes 49156
  103.4 9.2 %copy-start.6 = (s32[512,8]{0,1:T(8,128)S(1)}, s32[512,8]{0,1:T(8,128)}, u32[]{:S(2)}) copy-start(s32[512,8]{0,1:T(8,128)} %param.25) | copy-start | bytes 49156
  106.0 18.4 %all-to-all-start.1 = ((bf16[32,17,128]{2,1,0:T(8,128)(2,1)}), bf16[32,17,128]{2,1,0:T(8,128)(2,1)S(1)}, u32[]{:S(2)}, u32[]{:S(2)}) async-start(bf16[32,17,128]{2,1,0:T(8,128)(2,1)} %fusion.30), calls=%async_computation.1 | async-start | bytes 393216 | tf_op jit(solution)/shard_map/all_to_all | solution.py:113
  145.3 8.7 %copy-start.8 = (bf16[5,256,1536]{2,1,0:T(8,128)(2,1)S(1)}, bf16[5,256,1536]{2,1,0:T(8,128)(2,1)}, u32[]{:S(2)}) copy-start(bf16[5,256,1536]{2,1,0:T(8,128)(2,1)} %param.28) | copy-start | bytes 11796484
  159.1 20.9 %copy-start.2 = (bf16[512,192]{0,1:T(8,128)(2,1)S(1)}, bf16[512,192]{0,1:T(8,128)(2,1)}, u32[]{:S(2)}) copy-start(bf16[512,192]{0,1:T(8,128)(2,1)} %add_convert_fusion.1) | copy-start | bytes 589828
  159.1 20.6 %all-to-all-start.2 = ((bf16[8,512,192]{1,2,0:T(8,128)(2,1)}), bf16[8,512,192]{1,2,0:T(8,128)(2,1)S(1)}, u32[]{:S(2)}, u32[]{:S(2)}) async-start(bf16[8,512,192]{1,2,0:T(8,128)(2,1)} %bitcast.42), calls=%async_computation.2 | async-start | bytes 3145728 | tf_op jit(solution)/shard_map/all_to_all | solution.py:202
  (1 other events, 1.0 us)
Sparse Core Ops, SparseCore 0:
  11.5 46.6 all-gather.2
  104.2 39.1 all-gather.4
where the time goes:
time: 188 us
  waiting for transfers between devices  67.8 us (36%)
  starting transfers between devices  34.1 us (18%)
  blocking collectives  27 us (14%)
  matrix products  19.5 us (10%)
  other arithmetic  18.1 us (10%)
  between operations  14.6 us (8%)
  local copies, waits for them, and re-layouts  6.55 us (3%)
    all_to_all x1, blocking collectives, shards(): value_got = lax.all_to_all(value_parts, T, 0, 0, tiled=True)  27 us
    ppermute x7, starting transfers between devices, gather_rows_over_groups(): got.append(lax.ppermute(yfull, 'z', [(i, (i + k) % nz) for i in range(nz)]))  19.3 us
    ppermute x7, waiting for transfers between devices, gather_rows_over_groups(): got.append(lax.ppermute(yfull, 'z', [(i, (i + k) % nz) for i in range(nz)]))  18.6 us
    all_gather x1, waiting for transfers between devices, shards(): residual = lax.all_gather(residual_share, T, axis=1, tiled=True)  17.9 us
    all_to_all x1, waiting for transfers between devices, shards(): term_got = lax.all_to_all(term_parts, T, 0, 0, tiled=True)  16.3 us
    all_to_all x1, waiting for transfers between devices, place_cache_rows(): got = lax.all_to_all(packet, G, 0, 0, tiled=True)  11.6 us
    dot_general x1, matrix products, expert_terms(): jnp.einsum('td,edf->etf', normed, gateup, preferred_element_type=jnp.floa...  8.71 us
    all_to_all x1, starting transfers between devices, place_cache_rows(): got = lax.all_to_all(packet, G, 0, 0, tiled=True)  6.58 us
  transfers between devices with their start and end apart: 16, of which 9 were waited for; matrix products, arithmetic and copies ran while one was open for 7% of the time, Pallas kernels for 0%

commit v1 on v0

--- a/solution.py
+++ b/solution.py
@@ -1,8 +1,10 @@
+import functools
 import jax
 import jax.numpy as jnp
 from jax import lax
 from jax.sharding import Mesh
 from jax.sharding import PartitionSpec as P
+from jax.lax import all_to_all, axis_size
 
 HD = 64
 attn_scale = 0.015625
@@ -10,6 +12,17 @@
 rope_base = 10000.0
 G = ("z", "yh", "c")
 T = ("yl", "x")
+
+
+def flows_part(z_in, named_axis):
+    r2 = axis_size(named_axis)
+    carry_in = jnp.stack(r2 * [z_in], axis=0)
+    met_up = all_to_all(carry_in, named_axis, 0, 0)
+    h_now = jnp.concatenate(met_up, axis=1)
+    return h_now
+
+
+pass_body = functools.partial(flows_part, named_axis=T)
 
 
 def rms_scale(values, gain_row):
@@ -188,7 +201,7 @@
     residual_share, own_rows, cache_slots = lax.optimization_barrier(
         (residual_share, own_rows, cache_slots)
     )
-    residual = lax.all_gather(residual_share, T, axis=1, tiled=True)
+    residual = pass_body(residual_share)
     paged_rows = place_cache_rows(own_rows, cache_slots, group_rank)
     residual, paged_rows = lax.optimization_barrier((residual, paged_rows))
     normed = rms_scale(residual, gain_forward)

time: 188 us -> 199 us (1.059); the launches traced: 188 us -> 195 us
  blocking collectives: 27 us -> 45.1 us
  waiting for transfers between devices: 67.8 us -> 61.8 us
  starting transfers between devices: 34.1 us -> 31.1 us
  other arithmetic: 18.1 us -> 15.5 us
    all_to_all x0 -> x1, blocking collectives: none -> 18 us  [place_cache_rows(): got = lax.all_to_all(packet, G, 0, 0, tiled=True)]
    all_gather x1 -> x0, waiting for transfers between devices: 17.9 us -> none  [shards(): residual = lax.all_gather(residual_share, T, axis=1, tiled=True)]
    all_to_all x1, waiting for transfers between devices: 11.6 us -> 19.1 us  [flows_part(): met_up = all_to_all(carry_in, named_axis, 0, 0)]
    all_to_all x1, waiting for transfers between devices: 16.3 us -> 20.8 us  [shards(): term_got = lax.all_to_all(term_parts, T, 0, 0, tiled=True)]
    all_to_all x1, starting transfers between devices: 6.58 us -> 3.8 us  [flows_part(): met_up = all_to_all(carry_in, named_axis, 0, 0)]
  transfers between devices with their start and end apart: 16 -> 15, of which waited for: 9 -> 8; matrix products, arithmetic and copies ran while one was open for 7% -> 6% of each run, Pallas kernels for 0% -> 0%
where the time goes in v1:
time: 199 us; the launch traced here: 195 us
  waiting for transfers between devices  61.8 us (31%)
  blocking collectives  45.1 us (23%)
  starting transfers between devices  31.1 us (16%)
  matrix products  19 us (10%)
  other arithmetic  15.5 us (8%)
  between operations  14.6 us (7%)
  local copies, waits for them, and re-layouts  8.23 us (4%)
    all_to_all x1, blocking collectives, shards(): value_got = lax.all_to_all(value_parts, T, 0, 0, tiled=True)  27.1 us
    all_to_all x1, waiting for transfers between devices, shards(): term_got = lax.all_to_all(term_parts, T, 0, 0, tiled=True)  20.8 us
    ppermute x7, starting transfers between devices, gather_rows_over_groups(): got.append(lax.ppermute(yfull, 'z', [(i, (i + k) % nz) for i in range(nz)]))  19.3 us
    all_to_all x1, waiting for transfers between devices, flows_part(): met_up = all_to_all(carry_in, named_axis, 0, 0)  19.1 us
    ppermute x7, waiting for transfers between devices, gather_rows_over_groups(): got.append(lax.ppermute(yfull, 'z', [(i, (i + k) % nz) for i in range(nz)]))  18.6 us
    all_to_all x1, blocking collectives, place_cache_rows(): got = lax.all_to_all(packet, G, 0, 0, tiled=True)  18 us
    dot_general x1, matrix products, expert_terms(): jnp.einsum('td,edf->etf', normed, gateup, preferred_element_type=jnp.floa...  8.29 us
  transfers between devices with their start and end apart: 15, of which 8 were waited for; matrix products, arithmetic and copies ran while one was open for 6% of the time, Pallas kernels for 0%

profile of v1, /device:TPU:32, one launch (start us, length us, event | category | flops | bytes accessed | tf_op | source)
XLA Modules:
  0.0 195.3 jit_solution(6806177817256361713)
XLA Ops:
  9.7 1.7 pad_maximum_fusion.1
  16.9 3.3 %collective-permute-start.1 = (bf16[2,48,320]{2,1,0:T(8,128)(2,1)S(1)}, bf16[2,48,320]{2,1,0:T(8,128)(2,1)S(1)}, u32[]{:S(2)}, u32[]{:S(2)}) collective-permute-start(bf16[2,48,320]{2,1,0:T(8,128)(2,1)S(1)} %maximum_select_fusion.3), channel_id=1, source_target_pairs={{0,16},{16,0},{1,17},{17,1},{2,18},{18,2},{3,19},{19,3},{4,20},{20... | collective-permute-start | bytes 184328 | tf_op jit(solution)/shard_map/ppermute | solution.py:89
  20.2 2.9 %collective-permute-done.1 = bf16[2,48,320]{2,1,0:T(8,128)(2,1)S(1)} collective-permute-done((bf16[2,48,320]{2,1,0:T(8,128)(2,1)S(1)}, bf16[2,48,320]{2,1,0:T(8,128)(2,1)S(1)}, u32[]{:S(2)}, u32[]{:S(2)}) %collective-permute-start.1) | collective-permute-done | bytes 61472 | tf_op jit(solution)/shard_map/ppermute | solution.py:89
  23.2 2.0 %collective-permute-start.2 = (bf16[2,2,48,320]{3,2,1,0:T(8,128)(2,1)S(1)}, bf16[2,2,48,320]{3,2,1,0:T(8,128)(2,1)S(1)}, u32[]{:S(2)}, u32[]{:S(2)}) collective-permute-start(bf16[2,2,48,320]{3,2,1,0:T(8,128)(2,1)S(1)} %maximum_select_fusion.1), channel_id=1, source_target_pairs={{0,32},{32,64},{64,96},{96,128},{128,160},{160,192},{192,224},{224... | collective-permute-start | bytes 368648 | tf_op jit(solution)/shard_map/ppermute | solution.py:95
  25.2 4.6 %collective-permute-start.3 = (bf16[2,2,48,320]{3,2,1,0:T(8,128)(2,1)S(1)}, bf16[2,2,48,320]{3,2,1,0:T(8,128)(2,1)S(1)}, u32[]{:S(2)}, u32[]{:S(2)}) collective-permute-start(bf16[2,2,48,320]{3,2,1,0:T(8,128)(2,1)S(1)} %maximum_select_fusion.1), channel_id=1, source_target_pairs={{0,64},{32,96},{64,128},{96,160},{128,192},{160,224},{192,0},{224,... | collective-permute-start | bytes 368648 | tf_op jit(solution)/shard_map/ppermute | solution.py:95
  29.8 1.9 collective-permute-start.4
  33.1 3.0 %collective-permute-start.6 = (bf16[2,2,48,320]{3,2,1,0:T(8,128)(2,1)S(1)}, bf16[2,2,48,320]{3,2,1,0:T(8,128)(2,1)S(1)}, u32[]{:S(2)}, u32[]{:S(2)}) collective-permute-start(bf16[2,2,48,320]{3,2,1,0:T(8,128)(2,1)S(1)} %maximum_select_fusion.1), channel_id=1, source_target_pairs={{0,160},{32,192},{64,224},{96,0},{128,32},{160,64},{192,96},{224,1... | collective-permute-start | bytes 368648 | tf_op jit(solution)/shard_map/ppermute | solution.py:95
  36.2 2.5 %collective-permute-start.7 = (bf16[2,2,48,320]{3,2,1,0:T(8,128)(2,1)S(1)}, bf16[2,2,48,320]{3,2,1,0:T(8,128)(2,1)S(1)}, u32[]{:S(2)}, u32[]{:S(2)}) collective-permute-start(bf16[2,2,48,320]{3,2,1,0:T(8,128)(2,1)S(1)} %maximum_select_fusion.1), channel_id=1, source_target_pairs={{0,192},{32,224},{64,0},{96,32},{128,64},{160,96},{192,128},{224,1... | collective-permute-start | bytes 368648 | tf_op jit(solution)/shard_map/ppermute | solution.py:95
  40.0 3.8 %collective-permute-start.8 = (bf16[2,2,48,320]{3,2,1,0:T(8,128)(2,1)S(1)}, bf16[2,2,48,320]{3,2,1,0:T(8,128)(2,1)S(1)}, u32[]{:S(2)}, u32[]{:S(2)}) collective-permute-start(bf16[2,2,48,320]{3,2,1,0:T(8,128)(2,1)S(1)} %maximum_select_fusion.1), channel_id=1, source_target_pairs={{0,224},{32,0},{64,32},{96,64},{128,96},{160,128},{192,160},{224,1... | collective-permute-start | bytes 368648 | tf_op jit(solution)/shard_map/ppermute | solution.py:95
  43.9 9.9 %collective-permute-done.4 = bf16[2,2,48,320]{3,2,1,0:T(8,128)(2,1)S(1)} collective-permute-done((bf16[2,2,48,320]{3,2,1,0:T(8,128)(2,1)S(1)}, bf16[2,2,48,320]{3,2,1,0:T(8,128)(2,1)S(1)}, u32[]{:S(2)}, u32[]{:S(2)}) %collective-permute-start.4) | collective-permute-done | bytes 122912 | tf_op jit(solution)/shard_map/ppermute | solution.py:95
  53.9 6.0 %collective-permute-done.7 = bf16[2,2,48,320]{3,2,1,0:T(8,128)(2,1)S(1)} collective-permute-done((bf16[2,2,48,320]{3,2,1,0:T(8,128)(2,1)S(1)}, bf16[2,2,48,320]{3,2,1,0:T(8,128)(2,1)S(1)}, u32[]{:S(2)}, u32[]{:S(2)}) %collective-permute-start.7) | collective-permute-done | bytes 122912 | tf_op jit(solution)/shard_map/ppermute | solution.py:95
  62.6 1.9 fusion.2
  64.6 1.7 convert_reduce_fusion.2
  71.9 2.0 %fusion.17 = bf16[64,3,512]{2,0,1:T(8,128)(2,1)S(1)} fusion(f32[3,512]{1,0:T(4,128)S(1)} %fusion, f32[3,512]{1,0:T(4,128)S(1)} %get-tuple-element.51, f32[1024,512,3]{1,0,2:T(8,128)S(1)} %get-tuple-element.52, pred[512,1024]{0,1:T(8,128)(4,1)S(1)} %compare_and_fusion, bf16[1024,1,128]{0,2,1:T(8,128)(2,1)S(1)} %pad_maximum_fusion), kind=kOutput, calls=%fused_computation.31 | convolution fusion | flops 209289216 | bytes 7159808 | tf_op jit(solution)/shard_map/grqk,kgd->qgrd/dot_general | solution.py:63
  74.6 1.6 copy.67
  76.2 27.1 %all_to_all.20 = bf16[8,512,192]{1,2,0:T(8,128)(2,1)S(1)} all-to-all(bf16[8,512,192]{1,2,0:T(8,128)(2,1)} %bitcast.101), channel_id=1, replica_groups=mesh['z'=8,'yh'=2,'c'=2,'yl'=2,'x'=4] {'yl','x'}, dimensions={0} | all-to-all | bytes 3145728 | tf_op jit(solution)/shard_map/all_to_all | solution.py:198
  105.1 18.0 %all_to_all.21 = bf16[32,17,128]{2,1,0:T(8,128)(2,1)S(1)} all-to-all(bf16[32,17,128]{2,1,0:T(8,128)(2,1)S(1)} %fusion.30), channel_id=1, replica_groups=mesh['z'=8,'yh'=2,'c'=2,'yl'=2,'x'=4] {'z','yh','c'}, dimensions={0} | all-to-all | bytes 278528 | tf_op jit(solution)/shard_map/all_to_all | solution.py:126
  124.4 3.8 %all-to-all-start.1 = ((bf16[8,512,192]{1,2,0:T(8,128)(2,1)}), bf16[8,512,192]{1,2,0:T(8,128)(2,1)S(1)}, u32[]{:S(2)}, u32[]{:S(2)}) async-start(bf16[8,512,192]{1,2,0:T(8,128)(2,1)} %stack.111), calls=%async_computation.1 | async-start | bytes 3145728 | tf_op jit(solution)/shard_map/all_to_all | solution.py:20
  129.7 19.1 %all-to-all-done.1 = bf16[8,512,192]{1,2,0:T(8,128)(2,1)S(1)} async-done(((bf16[8,512,192]{1,2,0:T(8,128)(2,1)}), bf16[8,512,192]{1,2,0:T(8,128)(2,1)S(1)}, u32[]{:S(2)}, u32[]{:S(2)}) %all-to-all-start.1) | async-done | bytes 1572896 | tf_op jit(solution)/shard_map/all_to_all | solution.py:20
  149.2 8.3 %convolution_bitcast_fusion = f32[5,512,512]{2,1,0:T(8,128)S(1)} fusion(bf16[5,1536,512]{2,1,0:T(8,128)(2,1)} %param.27, bf16[512,1536]{0,1:T(8,128)(2,1)S(1)} %bitcast.100, f32[1536]{0:T(1024)S(1)} %get-tuple-element.37, f32[512]{0:T(512)S(1)} %add_rsqrt_fusion), kind=kOutput, calls=%fused_computation.24 | convolution fusion | flops 4029677568 | bytes 14688256 | tf_op jit(solution)/shard_map/td,edf->etf/dot_general | solution.py:75
  157.5 3.5 %multiply_reduce_fusion = bf16[512,1536]{1,0:T(8,128)(2,1)S(1)} fusion(bf16[5,256,1536]{2,1,0:T(8,128)(2,1)S(1)} %copy-done.9, f32[5,512]{1,0:T(8,128)S(1)} %bitcast.115, f32[5,512,512]{2,1,0:T(8,128)S(1)} %convolution_bitcast_fusion), kind=kOutput, calls=%fused_computation.1 | convolution fusion | flops 2024275968 | bytes 10758144 | tf_op jit(solution)/shard_map/etf,efd->etd/dot_general | solution.py:79
  161.0 1.6 copy.75
  162.6 3.6 %all-to-all-start.3 = ((bf16[8,512,192]{1,2,0:T(8,128)(2,1)}), bf16[8,512,192]{1,2,0:T(8,128)(2,1)S(1)}, u32[]{:S(2)}, u32[]{:S(2)}) async-start(bf16[8,512,192]{1,2,0:T(8,128)(2,1)} %bitcast.44), calls=%async_computation.3 | async-start | bytes 3145728 | tf_op jit(solution)/shard_map/all_to_all | solution.py:215
  166.8 20.8 %all-to-all-done.3 = bf16[8,512,192]{1,2,0:T(8,128)(2,1)S(1)} async-done(((bf16[8,512,192]{1,2,0:T(8,128)(2,1)}), bf16[8,512,192]{1,2,0:T(8,128)(2,1)S(1)}, u32[]{:S(2)}, u32[]{:S(2)}) %all-to-all-start.3) | async-done | bytes 1572896 | tf_op jit(solution)/shard_map/all_to_all | solution.py:215
  (110 shorter events, 26.1 us)
Async XLA Ops:
  7.2 66.8 %copy-start = (bf16[192,1536]{1,0:T(8,128)(2,1)S(1)}, bf16[192,1536]{1,0:T(8,128)(2,1)}, u32[]{:S(2)}) copy-start(bf16[192,1536]{1,0:T(8,128)(2,1)} %param.24) | copy-start | bytes 1769476
  7.2 55.4 %all-gather.2.cloned.1.call-start = ((), (), s32[]{:S(2)}) async-start(), calls=%async_computation.4 | async-start | bytes 2211840 | tf_op jit(solution)/shard_map/all_gather | solution.py:160
  8.1 8.8 %collective-permute-start = (bf16[48,320]{1,0:T(8,128)(2,1)S(1)}, bf16[48,320]{1,0:T(8,128)(2,1)S(1)}, u32[]{:S(2)}, u32[]{:S(2)}) collective-permute-start(bf16[48,320]{1,0:T(8,128)(2,1)S(1)} %get-tuple-element.45), channel_id=1, source_target_pairs={{0,8},{8,0},{1,9},{9,1},{2,10},{10,2},{3,11},{11,3},{4,12},{12,4},... | collective-permute-start | bytes 92168 | tf_op jit(solution)/shard_map/ppermute | solution.py:86
  11.4 2.5 %collective-permute-start.10 = (s32[512]{0:T(512)}, s32[512]{0:T(512)S(1)}, u32[]{:S(2)}, u32[]{:S(2)}) collective-permute-start(s32[512]{0:T(512)} %param.18), channel_id=1, source_target_pairs={{0,8},{8,0},{1,9},{9,1},{2,10},{10,2},{3,11},{11,3},{4,12},{12,4},... | collective-permute-start | bytes 6152 | tf_op jit(solution)/shard_map/ppermute | solution.py:182
  12.0 2.7 %collective-permute-start.11 = (s32[512]{0:T(512)}, s32[512]{0:T(512)S(1)}, u32[]{:S(2)}, u32[]{:S(2)}) collective-permute-start(s32[512]{0:T(512)} %param.19), channel_id=1, source_target_pairs={{0,8},{8,0},{1,9},{9,1},{2,10},{10,2},{3,11},{11,3},{4,12},{12,4},... | collective-permute-start | bytes 6152 | tf_op jit(solution)/shard_map/ppermute | solution.py:182
  16.9 6.2 %collective-permute-start.1 = (bf16[2,48,320]{2,1,0:T(8,128)(2,1)S(1)}, bf16[2,48,320]{2,1,0:T(8,128)(2,1)S(1)}, u32[]{:S(2)}, u32[]{:S(2)}) collective-permute-start(bf16[2,48,320]{2,1,0:T(8,128)(2,1)S(1)} %maximum_select_fusion.3), channel_id=1, source_target_pairs={{0,16},{16,0},{1,17},{17,1},{2,18},{18,2},{3,19},{19,3},{4,20},{20... | collective-permute-start | bytes 184328 | tf_op jit(solution)/shard_map/ppermute | solution.py:89
  23.2 13.0 %collective-permute-start.2 = (bf16[2,2,48,320]{3,2,1,0:T(8,128)(2,1)S(1)}, bf16[2,2,48,320]{3,2,1,0:T(8,128)(2,1)S(1)}, u32[]{:S(2)}, u32[]{:S(2)}) collective-permute-start(bf16[2,2,48,320]{3,2,1,0:T(8,128)(2,1)S(1)} %maximum_select_fusion.1), channel_id=1, source_target_pairs={{0,32},{32,64},{64,96},{96,128},{128,160},{160,192},{192,224},{224... | collective-permute-start | bytes 368648 | tf_op jit(solution)/shard_map/ppermute | solution.py:95
  25.2 14.8 %collective-permute-start.3 = (bf16[2,2,48,320]{3,2,1,0:T(8,128)(2,1)S(1)}, bf16[2,2,48,320]{3,2,1,0:T(8,128)(2,1)S(1)}, u32[]{:S(2)}, u32[]{:S(2)}) collective-permute-start(bf16[2,2,48,320]{3,2,1,0:T(8,128)(2,1)S(1)} %maximum_select_fusion.1), channel_id=1, source_target_pairs={{0,64},{32,96},{64,128},{96,160},{128,192},{160,224},{192,0},{224,... | collective-permute-start | bytes 368648 | tf_op jit(solution)/shard_map/ppermute | solution.py:95
  29.8 24.0 %collective-permute-start.4 = (bf16[2,2,48,320]{3,2,1,0:T(8,128)(2,1)S(1)}, bf16[2,2,48,320]{3,2,1,0:T(8,128)(2,1)S(1)}, u32[]{:S(2)}, u32[]{:S(2)}) collective-permute-start(bf16[2,2,48,320]{3,2,1,0:T(8,128)(2,1)S(1)} %maximum_select_fusion.1), channel_id=1, source_target_pairs={{0,96},{32,128},{64,160},{96,192},{128,224},{160,0},{192,32},{224,... | collective-permute-start | bytes 368648 | tf_op jit(solution)/shard_map/ppermute | solution.py:95
  31.7 22.2 %collective-permute-start.5 = (bf16[2,2,48,320]{3,2,1,0:T(8,128)(2,1)S(1)}, bf16[2,2,48,320]{3,2,1,0:T(8,128)(2,1)S(1)}, u32[]{:S(2)}, u32[]{:S(2)}) collective-permute-start(bf16[2,2,48,320]{3,2,1,0:T(8,128)(2,1)S(1)} %maximum_select_fusion.1), channel_id=1, source_target_pairs={{0,128},{32,160},{64,192},{96,224},{128,0},{160,32},{192,64},{224,... | collective-permute-start | bytes 368648 | tf_op jit(solution)/shard_map/ppermute | solution.py:95
  33.1 20.8 %collective-permute-start.6 = (bf16[2,2,48,320]{3,2,1,0:T(8,128)(2,1)S(1)}, bf16[2,2,48,320]{3,2,1,0:T(8,128)(2,1)S(1)}, u32[]{:S(2)}, u32[]{:S(2)}) collective-permute-start(bf16[2,2,48,320]{3,2,1,0:T(8,128)(2,1)S(1)} %maximum_select_fusion.1), channel_id=1, source_target_pairs={{0,160},{32,192},{64,224},{96,0},{128,32},{160,64},{192,96},{224,1... | collective-permute-start | bytes 368648 | tf_op jit(solution)/shard_map/ppermute | solution.py:95
  36.2 23.7 %collective-permute-start.7 = (bf16[2,2,48,320]{3,2,1,0:T(8,128)(2,1)S(1)}, bf16[2,2,48,320]{3,2,1,0:T(8,128)(2,1)S(1)}, u32[]{:S(2)}, u32[]{:S(2)}) collective-permute-start(bf16[2,2,48,320]{3,2,1,0:T(8,128)(2,1)S(1)} %maximum_select_fusion.1), channel_id=1, source_target_pairs={{0,192},{32,224},{64,0},{96,32},{128,64},{160,96},{192,128},{224,1... | collective-permute-start | bytes 368648 | tf_op jit(solution)/shard_map/ppermute | solution.py:95
  40.0 21.4 %collective-permute-start.8 = (bf16[2,2,48,320]{3,2,1,0:T(8,128)(2,1)S(1)}, bf16[2,2,48,320]{3,2,1,0:T(8,128)(2,1)S(1)}, u32[]{:S(2)}, u32[]{:S(2)}) collective-permute-start(bf16[2,2,48,320]{3,2,1,0:T(8,128)(2,1)S(1)} %maximum_select_fusion.1), channel_id=1, source_target_pairs={{0,224},{32,0},{64,32},{96,64},{128,96},{160,128},{192,160},{224,1... | collective-permute-start | bytes 368648 | tf_op jit(solution)/shard_map/ppermute | solution.py:95
  62.6 3.7 %copy-start.1 = (bf16[520,1536]{0,1:T(8,128)(2,1)S(1)}, bf16[520,1536]{0,1:T(8,128)(2,1)}, u32[]{:S(2)}) copy-start(bf16[520,1536]{0,1:T(8,128)(2,1)} %all-gather.2.cloned.1.call-done) | copy-start | bytes 4792324
  67.6 1.1 copy-start.4
  67.6 1.1 copy-start.3
  67.6 1.6 collective-permute-start.9
  76.2 27.3 %copy-start.2 = (bf16[512,192]{0,1:T(8,128)(2,1)S(1)}, bf16[512,192]{0,1:T(8,128)(2,1)}, u32[]{:S(2)}) copy-start(bf16[512,192]{0,1:T(8,128)(2,1)} %param.17) | copy-start | bytes 589828
  103.2 1.0 copy-start.5
  123.1 5.2 %copy-start.6 = (f32[512,8]{0,1:T(8,128)S(1)}, f32[512,8]{0,1:T(8,128)}, u32[]{:S(2)}) copy-start(f32[512,8]{0,1:T(8,128)} %param.26) | copy-start | bytes 49156
  123.1 5.2 %copy-start.7 = (s32[512,8]{0,1:T(8,128)S(1)}, s32[512,8]{0,1:T(8,128)}, u32[]{:S(2)}) copy-start(s32[512,8]{0,1:T(8,128)} %param.25) | copy-start | bytes 49156
  124.4 24.4 %all-to-all-start.1 = ((bf16[8,512,192]{1,2,0:T(8,128)(2,1)}), bf16[8,512,192]{1,2,0:T(8,128)(2,1)S(1)}, u32[]{:S(2)}, u32[]{:S(2)}) async-start(bf16[8,512,192]{1,2,0:T(8,128)(2,1)} %stack.111), calls=%async_computation.1 | async-start | bytes 3145728 | tf_op jit(solution)/shard_map/all_to_all | solution.py:20
  149.2 8.3 %copy-start.9 = (bf16[5,256,1536]{2,1,0:T(8,128)(2,1)S(1)}, bf16[5,256,1536]{2,1,0:T(8,128)(2,1)}, u32[]{:S(2)}) copy-start(bf16[5,256,1536]{2,1,0:T(8,128)(2,1)} %param.28) | copy-start | bytes 11796484
  162.6 24.9 %all-to-all-start.3 = ((bf16[8,512,192]{1,2,0:T(8,128)(2,1)}), bf16[8,512,192]{1,2,0:T(8,128)(2,1)S(1)}, u32[]{:S(2)}, u32[]{:S(2)}) async-start(bf16[8,512,192]{1,2,0:T(8,128)(2,1)} %bitcast.44), calls=%async_computation.3 | async-start | bytes 3145728 | tf_op jit(solution)/shard_map/all_to_all | solution.py:215
  (1 other events, 0.7 us)
Sparse Core Ops, SparseCore 0:
  11.5 46.7 all-gather.1
